TPU v7x, 32 devices: a whole 2x2x4 slice. The times are simulated.
32 devices in a mesh: task: 2 (over y), row: 4 (over z), col: 4 (over x, core).
Axes of the slice: x: 2, y: 2, z: 4, core: 2. Of those that a mesh axis runs over, the one named last changes fastest.
Arguments:
- features: bfloat16 [164, 4096], P(None, ('task', 'row', 'col')), parts along dimension 1, may hold values from -6 to 6
- rung_index: int32 [4096], P(('task', 'row', 'col')), parts along dimension 0, may hold values from 0 to 3
- w_first: bfloat16 [164, 512], replicated, may hold values from -0.5 to 0.5
- b_first: float32 [512], replicated, may hold values from -4 to 4
- w_second: bfloat16 [512, 512], replicated, may hold values from -0.25 to 0.25
- b_second: float32 [512], replicated, may hold values from -4 to 4
- w_third: bfloat16 [512, 64], replicated, may hold values from -0.25 to 0.25
- targets: float32 [16, 4096], P(None, ('task', 'row', 'col')), parts along dimension 1, may hold values from -80 to 80
- fidelity_factor: float32 [8, 4], P('task'), parts along dimension 0, may hold values from -4 to 4
- inverse_scale: float32 [2], P('task'), parts along dimension 0, may hold values from 0.02 to 0.1
- noise_var: float32 [2], P('task'), parts along dimension 0, may hold values from 0.3 to 1
Outputs:
- solution: float32 [16, 4096], P(None, ('task', 'row', 'col')), parts along dimension 1
- residual: float32 [16, 4096], P(None, ('task', 'row', 'col')), parts along dimension 1
There are 2 independent parts, one for each index of `task`. A program takes and returns all parts, laid end to end along the dimension named above; an argument that names none is the same for every part. Nothing has to cross between parts.
All inputs are finite; a program needn't handle non-finite values.
Results may differ from a plain program's by a relative error of at most 0.012.
The roundings to bfloat16 on the way count: a program that leaves them out, or rounds other values in their place, can miss the bound.
Values may be sent and summed in bfloat16 or wider, within the bound.
No kernel may reach another device: no remote copies, remote signals or barrier semaphores. Data moves between devices by JAX's collectives and lax.ppermute only.
A program may use at most 64 MiB of HBM per device.

v0:
```python
import jax
import jax.numpy as jnp
from jax import lax
from jax.sharding import PartitionSpec as P

ITERS = 2


def fidelity_matrix(fidelity_factor):
    lower = jnp.tril(fidelity_factor)
    return jnp.dot(lower, lower.T, precision=lax.Precision.HIGHEST) + 0.5 * jnp.eye(
        fidelity_factor.shape[0], dtype=jnp.float32
    )


def left_product(weights, values):
    return lax.dot_general(
        weights, values, (((0,), (0,)), ((), ())), preferred_element_type=jnp.float32
    )


def outer_gram(left_side, right_side):
    return lax.dot_general(
        left_side, right_side, (((1,), (1,)), ((), ())), precision=lax.Precision.HIGHEST
    )


def solve_spd(matrix, right_side):
    return jax.scipy.linalg.cho_solve((jnp.linalg.cholesky(matrix), True), right_side)


def block_size(total_count, largest):
    chosen = min(total_count, largest)
    while total_count % chosen != 0:
        chosen = chosen - 1
    return chosen


def rung_fidelity(fidelity, rung_value):
    levels = jnp.arange(fidelity.shape[0], dtype=jnp.float32)
    onehot = (rung_value.astype(jnp.float32)[None, :] == levels[:, None]).astype(jnp.float32)
    return (jnp.dot(fidelity, onehot, precision=lax.Precision.HIGHEST), onehot)


def split_two(values):
    high = lax.reduce_precision(values, exponent_bits=8, mantissa_bits=7)
    return (high.astype(jnp.bfloat16), (values - high).astype(jnp.bfloat16))


def split_product(direction, kernel):
    count = direction.shape[0]
    d_high, d_low = split_two(direction)
    k_high, k_low = split_two(kernel)
    dims = (((1,), (1,)), ((), ()))
    by_high = lax.dot_general(
        jnp.concatenate([d_high, d_low], axis=0), k_high, dims, preferred_element_type=jnp.float32
    )
    by_low = lax.dot_general(d_high, k_low, dims, preferred_element_type=jnp.float32)
    return by_high[:count] + by_high[count:] + by_low


def kernel_image(embedding, squares, rung_onehot, col_fidelity, inverse_scale, direction):
    count = embedding.shape[1]
    row_block = block_size(count, 2048)
    col_block = block_size(count, 2048)
    levels = jnp.arange(col_fidelity.shape[0], dtype=jnp.float32)

    def one_row_block(block_number):
        first_row = block_number * row_block
        rows_embedding = lax.dynamic_slice_in_dim(embedding, first_row, row_block, 1)
        rows_squares = lax.dynamic_slice_in_dim(squares, first_row, row_block, 0)
        rows_fidelity = lax.dynamic_slice_in_dim(col_fidelity, first_row, row_block, 1)

        def one_col_block(running, column_number):
            first_col = column_number * col_block
            cols_embedding = lax.dynamic_slice_in_dim(embedding, first_col, col_block, 1)
            cols_squares = lax.dynamic_slice_in_dim(squares, first_col, col_block, 0)
            cols_fidelity = lax.dynamic_slice_in_dim(col_fidelity, first_col, col_block, 1)
            cols_direction = lax.dynamic_slice_in_dim(direction, first_col, col_block, 1)
            cols_onehot = lax.dynamic_slice_in_dim(rung_onehot, first_col, col_block, 1)
            inner = left_product(rows_embedding, cols_embedding)
            distance = rows_squares[:, None] + cols_squares[None, :] - 2.0 * inner
            radial = jnp.exp(-inverse_scale[0] * distance)
            by_rung = jnp.concatenate(
                [
                    cols_direction * cols_onehot[level][None, :]
                    for level in range(col_fidelity.shape[0])
                ],
                axis=0,
            )
            rung_products = split_product(by_rung, radial)
            rhs = direction.shape[0]
            contribution = rows_fidelity[0][None, :] * rung_products[:rhs]
            for level in range(1, col_fidelity.shape[0]):
                contribution = (
                    contribution
                    + rows_fidelity[level][None, :] * rung_products[level * rhs : (level + 1) * rhs]
                )
            return (running + contribution, None)

        start_value = jnp.zeros((direction.shape[0], row_block), jnp.float32)
        result, unused = lax.scan(
            one_col_block, start_value, jnp.arange(count // col_block, dtype=jnp.int32)
        )
        return result

    stacked = lax.map(one_row_block, jnp.arange(count // row_block, dtype=jnp.int32))
    return jnp.transpose(stacked, (1, 0, 2)).reshape(direction.shape[0], count)


def on_device(
    features,
    rung_index,
    w_first,
    b_first,
    w_second,
    b_second,
    w_third,
    targets,
    fidelity_factor,
    inverse_scale,
    noise_var,
):
    fidelity = fidelity_matrix(fidelity_factor)
    hidden_one = jax.nn.silu(left_product(w_first, features) + b_first[:, None]).astype(
        jnp.bfloat16
    )
    hidden_two = jax.nn.silu(left_product(w_second, hidden_one) + b_second[:, None]).astype(
        jnp.bfloat16
    )
    embedding = lax.reduce_precision(
        left_product(w_third, hidden_two), exponent_bits=8, mantissa_bits=7
    )
    rung_value = rung_index.astype(jnp.float32)
    own_count = targets.shape[1]
    own_first = (lax.axis_index("row") * lax.axis_size("col") + lax.axis_index("col")) * own_count
    emb_rows = embedding.shape[0]
    packed = jnp.concatenate([embedding, targets, rung_value[None, :]], axis=0)
    gathered = lax.all_gather(packed, ("row", "col"), axis=1, tiled=True)
    all_embedding = gathered[:emb_rows].astype(jnp.bfloat16)
    all_targets = gathered[emb_rows : emb_rows + targets.shape[0]]
    all_rung = gathered[emb_rows + targets.shape[0]]
    squares = jnp.sum(jnp.square(gathered[:emb_rows]), axis=0)
    col_fidelity, rung_onehot = rung_fidelity(fidelity, all_rung)
    solution = jnp.zeros_like(all_targets)
    residual = all_targets
    direction = all_targets
    gram = outer_gram(residual, residual)
    for iteration in range(ITERS):
        image = (
            kernel_image(
                all_embedding, squares, rung_onehot, col_fidelity, inverse_scale, direction
            )
            + noise_var[0] * direction
        )
        curvature = outer_gram(direction, image)
        step_matrix = solve_spd(curvature, gram)
        solution = solution + jnp.dot(step_matrix.T, direction, precision=lax.Precision.HIGHEST)
        residual = residual - jnp.dot(step_matrix.T, image, precision=lax.Precision.HIGHEST)
        if iteration + 1 < ITERS:
            new_gram = outer_gram(residual, residual)
            update_matrix = solve_spd(gram, new_gram)
            direction = residual + jnp.dot(
                update_matrix.T, direction, precision=lax.Precision.HIGHEST
            )
            gram = new_gram
    own_solution = lax.dynamic_slice_in_dim(solution, own_first, own_count, 1)
    own_residual = lax.dynamic_slice_in_dim(residual, own_first, own_count, 1)
    return (own_solution, own_residual)


def solution(mesh):
    placed = (
        P(None, ("task", "row", "col")),
        P(("task", "row", "col")),
        P(),
        P(),
        P(),
        P(),
        P(),
        P(None, ("task", "row", "col")),
        P("task", None),
        P("task"),
        P("task"),
    )
    return jax.shard_map(
        on_device,
        mesh=mesh,
        in_specs=placed,
        out_specs=(P(None, ("task", "row", "col")), P(None, ("task", "row", "col"))),
        check_vma=False,
    )
```

profile of v0, /device:TPU:0, one launch (start us, length us, event | category | flops | bytes accessed | tf_op | source)
XLA Modules:
  0.0 69.6 jit_solution(14056495379713091680)
XLA Ops:
  0.6 0.7 %convert_bitcast_fusion = f32[1,128]{1,0:T(1,128)S(1)} fusion(s32[128]{0:T(128)} %param.15), kind=kLoop, calls=%fused_computation.113 | loop fusion | flops 128 | bytes 1024 | tf_op jit(solution)/shard_map/broadcast_in_dim | solution.py:138
  1.4 1.2 %multiply_convert_fusion.1 = bf16[512,128]{1,0:T(8,128)(2,1)S(1)} fusion(bf16[164,512]{1,0:T(8,128)(2,1)} %param.16, bf16[164,128]{1,0:T(8,128)(2,1)} %param.14, f32[512]{0:T(512)} %param.17), kind=kOutput, calls=%fused_computation.36 | convolution fusion | flops 21889024 | bytes 343040 | tf_op jit(solution)/shard_map/dot_general | solution.py:17
  2.6 1.4 %fusion.2 = f32[64,128]{1,0:T(8,128)S(1)} fusion(bf16[512,64]{0,1:T(8,128)(2,1)} %param.20, bf16[512,128]{1,0:T(8,128)(2,1)S(1)} %multiply_convert_fusion.1, bf16[512,512]{1,0:T(8,128)(2,1)S(1)} %copy-done, f32[512]{0:T(512)} %param.19), kind=kOutput, calls=%fused_computation.12 | convolution fusion | flops 75898880 | bytes 755712 | tf_op jit(solution)/shard_map/dot_general | solution.py:17
  4.0 0.7 %pad_maximum_fusion.2 = f32[81,128]{1,0:T(8,128)S(1)} fusion(f32[1,128]{1,0:T(1,128)S(1)} %convert_bitcast_fusion, f32[16,128]{1,0:T(8,128)} %param.21, f32[64,128]{1,0:T(8,128)S(1)} %fusion.2), kind=kLoop, calls=%fused_computation.70 | loop fusion | flops 20736 | bytes 82944 | tf_op jit(solution)/shard_map/concatenate | solution.py:138
  4.7 25.3 %all_gather.3 = f32[81,2048]{1,0:T(8,128)S(1)} all-gather(f32[81,128]{1,0:T(8,128)S(1)} %pad_maximum_fusion.2), channel_id=1, replica_groups=mesh['task'=2,'row'=4,'col'=4] {'row','col'}, dimensions={1}, use_global_device_ids=true | all-gather | bytes 705024 | tf_op jit(solution)/shard_map/all_gather | solution.py:139
  29.9 0.2 fusion.27
  30.2 0.1 slice.170
  30.3 0.1 fusion.3
  31.1 5.7 %reduce-precision_convert_fusion = (bf16[2048,2048]{1,0:T(8,128)(2,1)S(1)}, bf16[2048,2048]{1,0:T(8,128)(2,1)S(1)}) fusion(f32[2048]{0:T(1024)S(1)} %multiply_reduce_fusion, f32[]{:T(128)} %bitcast.9, f32[81,2048]{1,0:T(8,128)S(1)} %all_gather.3), kind=kOutput, calls=%fused_computation.1 | convolution fusion | flops 570425344 | bytes 17055748 | tf_op jit(solution)/shard_map/while/body/eval_jaxpr/while/body/eval_jaxpr/dot_general | solution.py:17
  36.8 2.9 %fusion.5 = f32[128,2048]{1,0:T(8,128)S(1)} fusion(bf16[2048,2048]{1,0:T(8,128)(2,1)S(1)} %get-tuple-element.106, bf16[64,2048]{1,0:T(8,128)(2,1)S(1)} %get-tuple-element.132, bf16[64,2048]{1,0:T(8,128)(2,1)S(1)} %get-tuple-element.133), kind=kOutput, calls=%fused_computation.23 | convolution fusion | flops 1074790400 | bytes 9961472 | tf_op jit(solution)/shard_map/while/body/eval_jaxpr/while/body/eval_jaxpr/dot_general | solution.py:55
  39.7 2.7 %convolution_add_fusion.1 = f32[64,2048]{1,0:T(8,128)S(1)} fusion(bf16[64,2048]{1,0:T(8,128)(2,1)S(1)} %get-tuple-element.133, bf16[2048,2048]{1,0:T(8,128)(2,1)S(1)} %get-tuple-element.107, f32[128,2048]{1,0:T(8,128)S(1)} %fusion.5), kind=kOutput, calls=%fused_computation.5 | convolution fusion | flops 537133056 | bytes 10223616 | tf_op jit(solution)/shard_map/while/body/eval_jaxpr/while/body/eval_jaxpr/dot_general | solution.py:58
  42.4 0.1 copy-done.3
  43.2 0.1 convolution_add_fusion.5
  43.3 0.2 fusion.32
  43.5 0.1 fusion.19
  43.6 0.2 fusion.29
  43.8 0.1 copy.14
  43.9 1.5 %cholesky.59 = f32[16,16]{1,0:T(8,128)S(1)} custom-call(f32[16,16]{1,0:T(8,128)S(1)} %fusion.51), custom_call_target="Cholesky" | custom-call | tf_op jit(solution)/shard_map/jit(cholesky)/cholesky | solution.py:29
  45.5 0.6 compare_reduce_fusion.2
  46.1 0.6 fusion.34
  46.8 1.2 %custom-call.9 = f32[1,16,16]{1,2,0:T(8,128)S(1)} custom-call(f32[1,16,16]{2,1,0:T(8,128)S(1)} %fusion.34), custom_call_target="InvertDiagBlocksLowerTriangular" | custom-call | tf_op jit(solution)/shard_map/jit(_cho_solve)/triangular_solve | solution.py:29
  48.0 0.2 fusion.49
  48.2 0.1 fusion.47
  48.3 0.3 convolution_subtract_fusion
  48.7 0.2 fusion.60
  48.9 0.1 copy.15
  49.0 1.5 %cholesky.70 = f32[16,16]{1,0:T(8,128)S(1)} custom-call(f32[16,16]{1,0:T(8,128)S(1)} %fusion.46), custom_call_target="Cholesky" | custom-call | tf_op jit(solution)/shard_map/jit(cholesky)/cholesky | solution.py:29
  50.5 0.6 compare_reduce_fusion.1
  51.2 0.6 fusion.35
  51.8 1.2 %custom-call.10 = f32[1,16,16]{1,2,0:T(8,128)S(1)} custom-call(f32[1,16,16]{2,1,0:T(8,128)S(1)} %fusion.35), custom_call_target="InvertDiagBlocksLowerTriangular" | custom-call | tf_op jit(solution)/shard_map/jit(_cho_solve)/triangular_solve | solution.py:29
  53.1 0.2 fusion.44
  53.3 0.1 fusion.42
  53.4 0.4 broadcast_multiply_fusion.6
  53.8 0.1 fusion.4
  53.9 6.6 %fusion.9 = f32[128,2048]{1,0:T(8,128)S(1)} fusion(bf16[2048,2048]{1,0:T(8,128)(2,1)} %copy-done.3, bf16[64,2048]{1,0:T(8,128)(2,1)S(1)} %get-tuple-element.130, bf16[64,2048]{1,0:T(8,128)(2,1)S(1)} %get-tuple-element.131), kind=kOutput, calls=%fused_computation.28 | convolution fusion | flops 1074790400 | bytes 9961472 | tf_op jit(solution)/shard_map/while/body/eval_jaxpr/while/body/eval_jaxpr/dot_general | solution.py:55
  60.5 2.7 %convolution_add_fusion = f32[64,2048]{1,0:T(8,128)S(1)} fusion(bf16[64,2048]{1,0:T(8,128)(2,1)S(1)} %get-tuple-element.131, bf16[2048,2048]{1,0:T(8,128)(2,1)S(1)} %copy-done.2, f32[128,2048]{1,0:T(8,128)S(1)} %fusion.9), kind=kOutput, calls=%fused_computation.4 | convolution fusion | flops 537133056 | bytes 10223616 | tf_op jit(solution)/shard_map/while/body/eval_jaxpr/while/body/eval_jaxpr/dot_general | solution.py:58
  63.2 0.2 fusion.61
  63.4 0.1 copy.16
  63.5 1.5 %cholesky.81 = f32[16,16]{1,0:T(8,128)S(1)} custom-call(f32[16,16]{1,0:T(8,128)S(1)} %fusion.41), custom_call_target="Cholesky" | custom-call | tf_op jit(solution)/shard_map/jit(cholesky)/cholesky | solution.py:29
  65.1 0.6 compare_reduce_fusion
  65.7 0.6 fusion.36
  66.4 1.2 %custom-call.11 = f32[1,16,16]{1,2,0:T(8,128)S(1)} custom-call(f32[1,16,16]{2,1,0:T(8,128)S(1)} %fusion.36), custom_call_target="InvertDiagBlocksLowerTriangular" | custom-call | tf_op jit(solution)/shard_map/jit(_cho_solve)/triangular_solve | solution.py:29
  67.6 0.2 fusion.39
  67.8 0.1 fusion.37
  68.0 0.3 fusion.63
  68.3 0.3 fusion.62
  68.6 0.3 fusion.25
  68.9 0.6 dynamic-slice_subtract_fusion
  (21 shorter events, 0.4 us)
Async XLA Ops:
  0.6 2.0 %copy-start = (bf16[512,512]{1,0:T(8,128)(2,1)S(1)}, bf16[512,512]{1,0:T(8,128)(2,1)}, u32[]{:S(2)}) copy-start(bf16[512,512]{1,0:T(8,128)(2,1)} %param.18) | copy-start | bytes 1572868
  36.8 5.6 %copy-start.1 = (bf16[2048,2048]{1,0:T(8,128)(2,1)}, bf16[2048,2048]{1,0:T(8,128)(2,1)S(1)}, u32[]{:S(2)}) copy-start(bf16[2048,2048]{1,0:T(8,128)(2,1)S(1)} %get-tuple-element.107) | copy-start | bytes 25165828
  36.8 5.7 %copy-start.3 = (bf16[2048,2048]{1,0:T(8,128)(2,1)}, bf16[2048,2048]{1,0:T(8,128)(2,1)S(1)}, u32[]{:S(2)}) copy-start(bf16[2048,2048]{1,0:T(8,128)(2,1)S(1)} %get-tuple-element.106) | copy-start | bytes 25165828
  36.8 6.3 %copy-start.4 = (f32[4,4]{1,0:T(4,128)S(1)}, f32[4,4]{1,0:T(4,128)}, u32[]{:S(2)}) copy-start(f32[4,4]{1,0:T(4,128)} %param.22) | copy-start | bytes 196
  53.1 7.4 %copy-start.2 = (bf16[2048,2048]{1,0:T(8,128)(2,1)S(1)}, bf16[2048,2048]{1,0:T(8,128)(2,1)}, u32[]{:S(2)}) copy-start(bf16[2048,2048]{1,0:T(8,128)(2,1)} %copy-done.1) | copy-start | bytes 25165828
where the time goes:
time: 69.9 us; the launch traced here: 69.6 us
  matrix products  27 us (39%)
  blocking collectives  25.3 us (36%)
  other arithmetic  14.6 us (21%)
  between operations  2.2 us (3%)
    all_gather x1, blocking collectives, on_device(): gathered = lax.all_gather(packed, ('row', 'col'), axis=1, tiled=True)  25.3 us
    dot_general x2, matrix products, split_product(): lax.dot_general(jnp.concatenate([d_high, d_low], axis=0), k_high, dims, p...  9.5 us
    dot_general x3, matrix products, left_product(): lax.dot_general(weights, values, (((0,), (0,)), ((), ())), preferred_elem...  8.27 us
    another operation x9, other arithmetic, solve_spd(): jnp.linalg.cholesky(matrix)  6.58 us
    another operation x6, other arithmetic, solve_spd(): jax.scipy.linalg.cho_solve((jnp.linalg.cholesky(matrix), True), right_side)  5.63 us
    dot_general x2, matrix products, split_product(): lax.dot_general(d_high, k_low, dims, preferred_element_type=jnp.float32)  5.32 us

commit v1 on v0

--- a/solution.py
+++ b/solution.py
@@ -4,6 +4,14 @@
 from jax.sharding import PartitionSpec as P
 
 ITERS = 2
+
+
+def tiled_gather(shard, axis, dim):
+    size = lax.axis_size(axis)
+    repeats = [size if d == dim else 1 for d in range(shard.ndim)]
+    return lax.all_to_all(
+        jnp.tile(shard, repeats), axis, split_axis=dim, concat_axis=dim, tiled=True
+    )
 
 
 def fidelity_matrix(fidelity_factor):
@@ -136,7 +144,7 @@
     own_first = (lax.axis_index("row") * lax.axis_size("col") + lax.axis_index("col")) * own_count
     emb_rows = embedding.shape[0]
     packed = jnp.concatenate([embedding, targets, rung_value[None, :]], axis=0)
-    gathered = lax.all_gather(packed, ("row", "col"), axis=1, tiled=True)
+    gathered = tiled_gather(packed, ("row", "col"), 1)
     all_embedding = gathered[:emb_rows].astype(jnp.bfloat16)
     all_targets = gathered[emb_rows : emb_rows + targets.shape[0]]
     all_rung = gathered[emb_rows + targets.shape[0]]

time: 69.9 us -> 69.2 us (0.990)
  blocking collectives: 25.3 us -> 0 us
  waiting for transfers between devices: 0 us -> 15.4 us
  starting transfers between devices: 0 us -> 7.39 us
  local copies, waits for them, and re-layouts: 0.51 us -> 1.34 us
  matrix products: 27 us -> 27.8 us
    all_gather x1 -> x0, blocking collectives: 25.3 us -> none  [on_device(): gathered = lax.all_gather(packed, ('row', 'col'), axis=1, tiled=True)]
    all_to_all x0 -> x1, waiting for transfers between devices: none -> 15.4 us  [tiled_gather(): lax.all_to_all(jnp.tile(shard, repeats), axis, split_axis=dim, concat_axi...]
    all_to_all x0 -> x1, starting transfers between devices: none -> 7.39 us  [tiled_gather(): lax.all_to_all(jnp.tile(shard, repeats), axis, split_axis=dim, concat_axi...]
    another operation x0 -> x1, local copies, waits for them, and re-layouts: none -> 0.9 us  [tiled_gather(): jnp.tile(shard, repeats)]
    dot_general x1, matrix products: 0.13 us -> 0.88 us  [fidelity_matrix(): jnp.dot(lower, lower.T, precision=lax.Precision.HIGHEST)]
  transfers between devices with their start and end apart: 0 -> 1, of which waited for: 0 -> 1; matrix products, arithmetic and copies ran while one was open for 0% -> 1% of each run, Pallas kernels for 0% -> 0%
where the time goes in v1:
time: 69.2 us; the launch traced here: 68.8 us
  matrix products  27.8 us (40%)
  waiting for transfers between devices  15.4 us (22%)
  other arithmetic  14.6 us (21%)
  starting transfers between devices  7.39 us (11%)
  between operations  2.18 us (3%)
  local copies, waits for them, and re-layouts  1.34 us (2%)
    all_to_all x1, waiting for transfers between devices, tiled_gather(): lax.all_to_all(jnp.tile(shard, repeats), axis, split_axis=dim, concat_axi...  15.4 us
    dot_general x2, matrix products, split_product(): lax.dot_general(jnp.concatenate([d_high, d_low], axis=0), k_high, dims, p...  9.51 us
    dot_general x3, matrix products, left_product(): lax.dot_general(weights, values, (((0,), (0,)), ((), ())), preferred_elem...  8.3 us
    all_to_all x1, starting transfers between devices, tiled_gather(): lax.all_to_all(jnp.tile(shard, repeats), axis, split_axis=dim, concat_axi...  7.39 us
    another operation x9, other arithmetic, solve_spd(): jnp.linalg.cholesky(matrix)  6.52 us
    another operation x6, other arithmetic, solve_spd(): jax.scipy.linalg.cho_solve((jnp.linalg.cholesky(matrix), True), right_side)  5.63 us
    dot_general x2, matrix products, split_product(): lax.dot_general(d_high, k_low, dims, preferred_element_type=jnp.float32)  5.32 us
  transfers between devices with their start and end apart: 1, of which 1 were waited for; matrix products, arithmetic and copies ran while one was open for 1% of the time, Pallas kernels for 0%

profile of v1, /device:TPU:0, one launch (start us, length us, event | category | flops | bytes accessed | tf_op | source)
XLA Modules:
  0.0 68.8 jit_solution(6360241354419702214)
XLA Ops:
  0.6 0.7 %convert_bitcast_fusion = f32[1,128]{1,0:T(1,128)S(1)} fusion(s32[128]{0:T(128)} %param.15), kind=kLoop, calls=%fused_computation.124 | loop fusion | flops 128 | bytes 1024 | tf_op jit(solution)/shard_map/broadcast_in_dim | solution.py:146
  1.4 1.2 %multiply_convert_fusion.1 = bf16[512,128]{1,0:T(8,128)(2,1)S(1)} fusion(bf16[164,512]{1,0:T(8,128)(2,1)} %param.16, bf16[164,128]{1,0:T(8,128)(2,1)} %param.14, f32[512]{0:T(512)} %param.17), kind=kOutput, calls=%fused_computation.40 | convolution fusion | flops 21889024 | bytes 343040 | tf_op jit(solution)/shard_map/dot_general | solution.py:25
  2.6 1.4 %fusion.2 = f32[64,128]{1,0:T(8,128)S(1)} fusion(bf16[512,64]{0,1:T(8,128)(2,1)} %param.20, bf16[512,128]{1,0:T(8,128)(2,1)S(1)} %multiply_convert_fusion.1, bf16[512,512]{1,0:T(8,128)(2,1)S(1)} %copy-done, f32[512]{0:T(512)} %param.19), kind=kOutput, calls=%fused_computation.12 | convolution fusion | flops 75898880 | bytes 755712 | tf_op jit(solution)/shard_map/dot_general | solution.py:25
  4.0 0.7 %pad_maximum_fusion.2 = f32[81,128]{1,0:T(8,128)S(1)} fusion(f32[1,128]{1,0:T(1,128)S(1)} %convert_bitcast_fusion, f32[16,128]{1,0:T(8,128)} %param.21, f32[64,128]{1,0:T(8,128)S(1)} %fusion.2), kind=kLoop, calls=%fused_computation.81 | loop fusion | flops 20736 | bytes 82944 | tf_op jit(solution)/shard_map/concatenate | solution.py:146
  4.7 0.9 %tile.2 = f32[81,16,128]{2,0,1:T(8,128)} broadcast(f32[81,128]{1,0:T(8,128)S(1)} %pad_maximum_fusion.2), dimensions={0,2} | broadcast | bytes 705024 | tf_op jit(solution)/shard_map/tile | solution.py:13
  5.6 7.4 %all-to-all-start = ((f32[81,16,128]{2,0,1:T(8,128)}), f32[81,16,128]{2,0,1:T(8,128)S(1)}, u32[]{:S(2)}, u32[]{:S(2)}) async-start(f32[81,16,128]{2,0,1:T(8,128)} %tile.2), calls=%async_computation | async-start | bytes 1441792 | tf_op jit(solution)/shard_map/all_to_all | solution.py:12
  14.3 0.9 %convolution_add_fusion.5 = f32[4,4]{1,0:T(4,128)S(1)} fusion(f32[4,4]{1,0:T(4,128)} %param.22), kind=kOutput, calls=%fused_computation.14 | convolution fusion | flops 848 | bytes 128 | tf_op jit(solution)/shard_map/dot_general | solution.py:19
  15.2 15.4 %all-to-all-done = f32[81,16,128]{2,0,1:T(8,128)S(1)} async-done(((f32[81,16,128]{2,0,1:T(8,128)}), f32[81,16,128]{2,0,1:T(8,128)S(1)}, u32[]{:S(2)}, u32[]{:S(2)}) %all-to-all-start) | async-done | bytes 663584 | tf_op jit(solution)/shard_map/all_to_all | solution.py:12
  30.7 0.2 fusion.42
  30.9 0.1 fusion.3
  31.1 5.7 %reduce-precision_convert_fusion = (bf16[2048,2048]{1,0:T(8,128)(2,1)S(1)}, bf16[2048,2048]{1,0:T(8,128)(2,1)S(1)}) fusion(f32[2048]{0:T(1024)S(1)} %bitcast.147, f32[]{:T(128)} %bitcast.9, f32[81,16,128]{2,0,1:T(8,128)S(1)} %all-to-all-done), kind=kOutput, calls=%fused_computation.1 | convolution fusion | flops 570425344 | bytes 17055748 | tf_op jit(solution)/shard_map/while/body/eval_jaxpr/while/body/eval_jaxpr/dot_general | solution.py:25
  36.8 2.9 %fusion.5 = f32[128,2048]{1,0:T(8,128)S(1)} fusion(bf16[2048,2048]{1,0:T(8,128)(2,1)S(1)} %get-tuple-element.106, bf16[64,2048]{1,0:T(8,128)(2,1)S(1)} %get-tuple-element.128, bf16[64,2048]{1,0:T(8,128)(2,1)S(1)} %get-tuple-element.129), kind=kOutput, calls=%fused_computation.24 | convolution fusion | flops 1074790400 | bytes 9961472 | tf_op jit(solution)/shard_map/while/body/eval_jaxpr/while/body/eval_jaxpr/dot_general | solution.py:63
  39.7 2.7 %convolution_add_fusion.1 = f32[64,2048]{1,0:T(8,128)S(1)} fusion(bf16[64,2048]{1,0:T(8,128)(2,1)S(1)} %get-tuple-element.129, bf16[2048,2048]{1,0:T(8,128)(2,1)S(1)} %get-tuple-element.107, f32[128,2048]{1,0:T(8,128)S(1)} %fusion.5), kind=kOutput, calls=%fused_computation.5 | convolution fusion | flops 537133056 | bytes 10223616 | tf_op jit(solution)/shard_map/while/body/eval_jaxpr/while/body/eval_jaxpr/dot_general | solution.py:66
  42.3 0.1 copy-done.3
  42.5 0.2 fusion.20
  42.8 0.1 copy.21
  42.9 1.5 %cholesky.59 = f32[16,16]{1,0:T(8,128)S(1)} custom-call(f32[16,16]{1,0:T(8,128)S(1)} %fusion.61), custom_call_target="Cholesky" | custom-call | tf_op jit(solution)/shard_map/jit(cholesky)/cholesky | solution.py:37
  44.4 0.6 compare_reduce_fusion.2
  45.1 0.6 fusion.44
  45.7 1.2 %custom-call.9 = f32[1,16,16]{1,2,0:T(8,128)S(1)} custom-call(f32[1,16,16]{2,1,0:T(8,128)S(1)} %fusion.44), custom_call_target="InvertDiagBlocksLowerTriangular" | custom-call | tf_op jit(solution)/shard_map/jit(_cho_solve)/triangular_solve | solution.py:37
  46.9 0.2 convolution_bitcast_fusion
  47.2 0.1 copy.22
  47.3 0.3 fusion.59
  47.5 0.1 fusion.57
  47.7 0.3 convolution_subtract_fusion
  48.0 0.2 fusion.70
  48.3 1.5 %cholesky.70 = f32[16,16]{1,0:T(8,128)S(1)} custom-call(f32[16,16]{1,0:T(8,128)S(1)} %fusion.56), custom_call_target="Cholesky" | custom-call | tf_op jit(solution)/shard_map/jit(cholesky)/cholesky | solution.py:37
  49.8 0.6 compare_reduce_fusion.1
  50.4 0.6 fusion.45
  51.1 1.2 %custom-call.10 = f32[1,16,16]{1,2,0:T(8,128)S(1)} custom-call(f32[1,16,16]{2,1,0:T(8,128)S(1)} %fusion.45), custom_call_target="InvertDiagBlocksLowerTriangular" | custom-call | tf_op jit(solution)/shard_map/jit(_cho_solve)/triangular_solve | solution.py:37
  52.3 0.2 fusion.54
  52.5 0.1 fusion.52
  52.6 0.4 broadcast_multiply_fusion.3
  53.0 0.1 fusion.4
  53.1 6.6 %fusion.9 = f32[128,2048]{1,0:T(8,128)S(1)} fusion(bf16[2048,2048]{1,0:T(8,128)(2,1)} %copy-done.3, bf16[64,2048]{1,0:T(8,128)(2,1)S(1)} %get-tuple-element.108, bf16[64,2048]{1,0:T(8,128)(2,1)S(1)} %get-tuple-element.109), kind=kOutput, calls=%fused_computation.29 | convolution fusion | flops 1074790400 | bytes 9961472 | tf_op jit(solution)/shard_map/while/body/eval_jaxpr/while/body/eval_jaxpr/dot_general | solution.py:63
  59.7 2.7 %convolution_add_fusion = f32[64,2048]{1,0:T(8,128)S(1)} fusion(bf16[64,2048]{1,0:T(8,128)(2,1)S(1)} %get-tuple-element.109, bf16[2048,2048]{1,0:T(8,128)(2,1)S(1)} %copy-done.2, f32[128,2048]{1,0:T(8,128)S(1)} %fusion.9), kind=kOutput, calls=%fused_computation.4 | convolution fusion | flops 537133056 | bytes 10223616 | tf_op jit(solution)/shard_map/while/body/eval_jaxpr/while/body/eval_jaxpr/dot_general | solution.py:66
  62.5 0.2 fusion.71
  62.7 0.1 copy.23
  62.8 1.5 %cholesky.81 = f32[16,16]{1,0:T(8,128)S(1)} custom-call(f32[16,16]{1,0:T(8,128)S(1)} %fusion.51), custom_call_target="Cholesky" | custom-call | tf_op jit(solution)/shard_map/jit(cholesky)/cholesky | solution.py:37
  64.3 0.6 compare_reduce_fusion
  65.0 0.6 fusion.46
  65.6 1.2 %custom-call.11 = f32[1,16,16]{1,2,0:T(8,128)S(1)} custom-call(f32[1,16,16]{2,1,0:T(8,128)S(1)} %fusion.46), custom_call_target="InvertDiagBlocksLowerTriangular" | custom-call | tf_op jit(solution)/shard_map/jit(_cho_solve)/triangular_solve | solution.py:37
  66.9 0.2 fusion.49
  67.1 0.1 fusion.47
  67.2 0.3 fusion.73
  67.5 0.3 fusion.72
  67.9 0.3 fusion.18
  68.2 0.6 dynamic-slice_subtract_fusion
  (21 shorter events, 0.5 us)
Async XLA Ops:
  0.6 2.0 %copy-start = (bf16[512,512]{1,0:T(8,128)(2,1)S(1)}, bf16[512,512]{1,0:T(8,128)(2,1)}, u32[]{:S(2)}) copy-start(bf16[512,512]{1,0:T(8,128)(2,1)} %param.18) | copy-start | bytes 1572868
  5.6 25.0 %all-to-all-start = ((f32[81,16,128]{2,0,1:T(8,128)}), f32[81,16,128]{2,0,1:T(8,128)S(1)}, u32[]{:S(2)}, u32[]{:S(2)}) async-start(f32[81,16,128]{2,0,1:T(8,128)} %tile.2), calls=%async_computation | async-start | bytes 1441792 | tf_op jit(solution)/shard_map/all_to_all | solution.py:12
  36.8 5.6 %copy-start.1 = (bf16[2048,2048]{1,0:T(8,128)(2,1)}, bf16[2048,2048]{1,0:T(8,128)(2,1)S(1)}, u32[]{:S(2)}) copy-start(bf16[2048,2048]{1,0:T(8,128)(2,1)S(1)} %get-tuple-element.107) | copy-start | bytes 25165828
  36.8 5.7 %copy-start.3 = (bf16[2048,2048]{1,0:T(8,128)(2,1)}, bf16[2048,2048]{1,0:T(8,128)(2,1)S(1)}, u32[]{:S(2)}) copy-start(bf16[2048,2048]{1,0:T(8,128)(2,1)S(1)} %get-tuple-element.106) | copy-start | bytes 25165828
  52.3 7.4 %copy-start.2 = (bf16[2048,2048]{1,0:T(8,128)(2,1)S(1)}, bf16[2048,2048]{1,0:T(8,128)(2,1)}, u32[]{:S(2)}) copy-start(bf16[2048,2048]{1,0:T(8,128)(2,1)} %copy-done.1) | copy-start | bytes 25165828
